TPU v7x, 128 devices: a whole 4x4x4 slice. The times are simulated.
128 devices in a mesh: dp: 128 (over y, z, x, core).
Axes of the slice: x: 4, y: 4, z: 4, core: 2. Of those that a mesh axis runs over, the one named last changes fastest.
Arguments:
- spikes: bfloat16 [512, 256, 256], P('dp'), may hold values from -6 to 6
- block_lists: int32 [512, 2], P('dp'), may hold values from 0 to 2047, as said below
- bin_counts: int32 [512], P('dp'), may hold values from 1 to 256, as said below
- readin_table: bfloat16 [2048, 128, 1024], P('dp'), may hold values from -0.375 to 0.375
- norm_gain: float32 [1024], replicated, may hold values from 0.1 to 1.9
- w_in: bfloat16 [1024, 2048], replicated, may hold values from -0.1875 to 0.1875
- w_out: bfloat16 [2048, 1024], replicated, may hold values from -0.125 to 0.125
- cotangent: bfloat16 [512, 256, 1024], P(None, 'dp'), may hold values from -6 to 6
Outputs:
- encoded: bfloat16 [512, 256, 1024], P(None, 'dp')
- readin_grad: bfloat16 [2048, 128, 1024], P('dp')
Inputs may be any that keep to these rules, and one draw needn't show every extreme that they name: `block_lists`: block k is held by device k // 16. The sessions of device d are d * 4 to (d + 1) * 4 - 1; of their 8 entries exactly 1 name blocks held by each of the devices d, d + 1, ..., d + 7, counted modulo the number of devices. `bin_counts`: among the sessions of every device one has all 256 bins valid.
All inputs are finite; a program needn't handle non-finite values.
Results may differ from a plain program's by a relative error of at most 0.0056.
Values may be sent and summed in bfloat16 or wider, within the bound.
No kernel may reach another device: no remote copies, remote signals or barrier semaphores. Data moves between devices by JAX's collectives and lax.ppermute only.
A program may use at most 128 MiB of HBM per device.

v0:
```python
import jax
import jax.numpy as jnp
from jax import lax
from jax.sharding import PartitionSpec as P

EPS = 1e-06


def from_behind(array, axis, by):
    count = lax.axis_size(axis)
    return lax.ppermute(array, axis, [(i, (i + by) % count) for i in range(count)])


def gelu_tanh(values):
    return jax.nn.gelu(values, approximate=True)


def encode_rows(latent_rows, norm_gain, w_in, w_out, cot_rows):
    inputs = latent_rows.astype(jnp.float32)
    mean_square = jnp.mean(inputs * inputs, axis=-1, keepdims=True)
    inverse_rms = lax.rsqrt(mean_square + EPS)
    normed = (inputs * inverse_rms * norm_gain).astype(jnp.bfloat16)
    hidden_pre = jnp.dot(normed, w_in, preferred_element_type=jnp.float32)
    activated, pullback = jax.vjp(gelu_tanh, hidden_pre)
    activated = activated.astype(jnp.bfloat16)
    encoded = (inputs + jnp.dot(activated, w_out, preferred_element_type=jnp.float32)).astype(
        jnp.bfloat16
    )
    grad_activated = lax.dot_general(
        cot_rows, w_out, (((1,), (1,)), ((), ())), preferred_element_type=jnp.float32
    )
    grad_hidden = pullback(grad_activated)[0].astype(jnp.bfloat16)
    grad_normed = lax.dot_general(
        grad_hidden, w_in, (((1,), (1,)), ((), ())), preferred_element_type=jnp.float32
    )
    scaled = grad_normed * norm_gain
    grad_inputs = inverse_rms * scaled - inputs * (
        inverse_rms * inverse_rms * inverse_rms
    ) * jnp.mean(scaled * inputs, axis=-1, keepdims=True)
    returned = (cot_rows.astype(jnp.float32) + grad_inputs).astype(jnp.bfloat16)
    return (encoded, returned)


def on_device(spikes, block_lists, bin_counts, readin_table, norm_gain, w_in, w_out, cotangent):
    devices = lax.axis_size("dp")
    me = lax.axis_index("dp")
    sessions_here, bins_all, unit_columns = spikes.shape
    table_rows, unit_block, latent_width = readin_table.shape
    blocks_per = unit_columns // unit_block
    slot_count = sessions_here * blocks_per
    near = slot_count

    flat_lists = block_lists.reshape(slot_count)
    offsets = jnp.mod(flat_lists // table_rows - me, devices)
    slot_ids = jnp.arange(slot_count, dtype=jnp.int32)
    match = offsets[None, :] == jnp.arange(near, dtype=jnp.int32)[:, None]
    slot_of = jnp.sum(jnp.where(match, slot_ids[None, :], 0), axis=1)

    all_lists = lax.all_gather(flat_lists, "dp", axis=0, tiled=False)
    sources = jnp.mod(me - jnp.arange(near, dtype=jnp.int32), devices)
    source_lists = jnp.take(all_lists, sources, axis=0)
    mine = (source_lists // table_rows) == me
    rows_in = jnp.sum(jnp.where(mine, jnp.mod(source_lists, table_rows), 0), axis=1)

    fetched = [lax.dynamic_slice_in_dim(readin_table, rows_in[0], 1, axis=0)]
    for offset in range(1, near):
        block = lax.dynamic_slice_in_dim(readin_table, rows_in[offset], 1, axis=0)
        fetched.append(from_behind(block, "dp", -offset))

    cot_here = lax.all_to_all(cotangent, "dp", split_axis=0, concat_axis=1, tiled=True)

    by_offset = jnp.concatenate(fetched, axis=0)
    by_slot = jnp.take(by_offset, offsets, axis=0)
    weights = by_slot.reshape(sessions_here, blocks_per * unit_block, latent_width)
    valid = (
        lax.broadcasted_iota(jnp.int32, (sessions_here, bins_all), 1) < bin_counts[:, None]
    ).astype(jnp.float32)[:, :, None]
    latent = jnp.einsum("stk,skd->std", spikes, weights, preferred_element_type=jnp.float32)
    latent = (latent * valid).astype(jnp.bfloat16)

    encoded, returned = encode_rows(
        latent.reshape(-1, latent_width),
        norm_gain,
        w_in,
        w_out,
        cot_here.reshape(-1, latent_width),
    )
    encoded_out = lax.all_to_all(
        encoded.reshape(sessions_here, bins_all, latent_width),
        "dp",
        split_axis=1,
        concat_axis=0,
        tiled=True,
    )

    grad_latent = (
        returned.reshape(sessions_here, bins_all, latent_width).astype(jnp.float32) * valid
    ).astype(jnp.bfloat16)
    slot_grads = jnp.einsum(
        "stk,std->skd", spikes, grad_latent, preferred_element_type=jnp.float32
    ).astype(jnp.bfloat16)
    slot_grads = slot_grads.reshape(slot_count, unit_block, latent_width)

    total = jnp.zeros((table_rows, unit_block, latent_width), jnp.float32)
    for offset in range(near):
        piece = lax.dynamic_slice_in_dim(slot_grads, slot_of[offset], 1, axis=0)
        if offset > 0:
            piece = from_behind(piece, "dp", offset)
        row = rows_in[offset]
        current = lax.dynamic_slice_in_dim(total, row, 1, axis=0)
        total = lax.dynamic_update_slice_in_dim(
            total, current + piece.astype(jnp.float32), row, axis=0
        )
    return (encoded_out, total.astype(jnp.bfloat16))


def solution(mesh):
    return jax.shard_map(
        on_device,
        mesh=mesh,
        in_specs=(
            P("dp", None, None),
            P("dp", None),
            P("dp"),
            P("dp", None, None),
            P(),
            P(),
            P(),
            P(None, "dp", None),
        ),
        out_specs=(P(None, "dp", None), P("dp", None, None)),
        check_vma=False,
    )
```

profile of v0, /device:TPU:1, one launch (start us, length us, event | category | flops | bytes accessed | tf_op | source)
XLA Modules:
  0.0 249.1 jit_solution(1851743815558147179)
XLA Ops:
  0.7 12.0 %all-to-all-start.1 = ((bf16[512,2,1024]{2,1,0:T(2,128)(2,1)}), bf16[512,2,1024]{2,1,0:T(2,128)(2,1)}, u32[]{:S(2)}, u32[]{:S(2)}) async-start(bf16[512,2,1024]{2,1,0:T(2,128)(2,1)} %param.15), calls=%async_computation.1 | async-start | bytes 4194304 | tf_op jit(solution)/shard_map/all_to_all | solution.py:70
  13.0 49.1 %all-gather = s32[128,1,8]{2,1,0:T(1,128)S(1)} all-gather(s32[1,1,8]{2,1,0:T(1,128)S(1)} %reshape.315), channel_id=1, replica_groups=mesh['dp'=128] {'dp'}, dimensions={0}, use_global_device_ids=true | all-gather | bytes 4128 | tf_op jit(solution)/shard_map/all_gather | solution.py:59
  78.8 2.5 %constant_dynamic-slice_fusion.7 = (bf16[1,128,1024]{2,1,0:T(8,128)(2,1)S(1)}, bf16[1,128,1024]{2,1,0:T(8,128)(2,1)S(1)}, bf16[1,128,1024]{2,1,0:T(8,128)(2,1)S(...) fusion(bf16[16,128,1024]{2,1,0:T(8,128)(2,1)} %param.11, ...), kind=kLoop, calls=%fused_computation.59 | loop fusion | bytes 4194336 | tf_op jit(solution)/shard_map/dynamic_slice | solution.py:67
  83.2 3.3 %collective-permute-start.4 = (bf16[1,128,1024]{2,1,0:T(8,128)(2,1)S(1)}, bf16[1,128,1024]{2,1,0:T(8,128)(2,1)S(1)}, u32[]{:S(2)}, u32[]{:S(2)}) collective-permute-start(bf16[1,128,1024]{2,1,0:T(8,128)(2,1)S(1)} %get-tuple-element.3), channel_id=1, source_target_pairs={{0,123},{1,124},{2,125},{3,126},{4,127},{5,0},{6,1},{7,2},{8,3},{9... | collective-permute-start | bytes 786440 | tf_op jit(solution)/shard_map/ppermute | solution.py:11
  103.7 3.4 %collective-permute-start.3 = (bf16[1,128,1024]{2,1,0:T(8,128)(2,1)S(1)}, bf16[1,128,1024]{2,1,0:T(8,128)(2,1)S(1)}, u32[]{:S(2)}, u32[]{:S(2)}) collective-permute-start(bf16[1,128,1024]{2,1,0:T(8,128)(2,1)S(1)} %get-tuple-element.4), channel_id=1, source_target_pairs={{0,124},{1,125},{2,126},{3,127},{4,0},{5,1},{6,2},{7,3},{8,4},{9,5... | collective-permute-start | bytes 786440 | tf_op jit(solution)/shard_map/ppermute | solution.py:11
  108.8 4.2 %collective-permute-start.5 = (bf16[1,128,1024]{2,1,0:T(8,128)(2,1)S(1)}, bf16[1,128,1024]{2,1,0:T(8,128)(2,1)S(1)}, u32[]{:S(2)}, u32[]{:S(2)}) collective-permute-start(bf16[1,128,1024]{2,1,0:T(8,128)(2,1)S(1)} %get-tuple-element.9), channel_id=1, source_target_pairs={{0,122},{1,123},{2,124},{3,125},{4,126},{5,127},{6,0},{7,1},{8,2},... | collective-permute-start | bytes 786440 | tf_op jit(solution)/shard_map/ppermute | solution.py:11
  115.9 3.2 %collective-permute-done.5 = bf16[1,128,1024]{2,1,0:T(8,128)(2,1)S(1)} collective-permute-done((bf16[1,128,1024]{2,1,0:T(8,128)(2,1)S(1)}, bf16[1,128,1024]{2,1,0:T(8,128)(2,1)S(1)}, u32[]{:S(2)}, u32[]{:S(2)}) %collective-permute-start.5) | collective-permute-done | bytes 262176 | tf_op jit(solution)/shard_map/ppermute | solution.py:11
  120.6 2.3 gather_fusion.1
  125.3 4.5 %fusion.53 = f32[1024,2048]{1,0:T(8,128)S(1)} fusion(bf16[1024,1024]{1,0:T(8,128)(2,1)S(1)} %fusion.10, bf16[1024,2048]{1,0:T(8,128)(2,1)S(1)} %copy-done.7), kind=kOutput, calls=%fused_computation.140 | convolution fusion | flops 4294967296 | bytes 14680064 | tf_op jit(solution)/shard_map/dot_general | solution.py:23
  129.8 5.5 %fusion.11 = bf16[1024,1024]{1,0:T(8,128)(2,1)S(1)} fusion(bf16[4,1024,256]{1,2,0:T(8,128)(2,1)S(1)} %get-tuple-element.34, bf16[2048,1024]{1,0:T(8,128)(2,1)S(1)} %copy-done.6, f32[1024,2048]{1,0:T(8,128)S(1)} %fusion.53), kind=kOutput, calls=%fused_computation.22 | convolution fusion | flops 4316987392 | bytes 16777216 | tf_op jit(solution)/shard_map/dot_general | solution.py:26
  135.4 2.9 %copy.27 = bf16[4,256,1024]{2,0,1:T(4,128)(2,1)} copy(bf16[4,256,1024]{2,1,0:T(8,128)(2,1)S(1)} %bitcast.81) | data formatting | bytes 4194304 | tf_op jit(solution)/shard_map/reshape | solution.py:89
  138.3 9.5 %all-to-all-start = ((bf16[4,256,1024]{2,0,1:T(4,128)(2,1)}), bf16[4,256,1024]{2,0,1:T(4,128)(2,1)}, u32[]{:S(2)}, u32[]{:S(2)}) async-start(bf16[4,256,1024]{2,0,1:T(4,128)(2,1)} %copy.27), calls=%async_computation | async-start | bytes 4194304 | tf_op jit(solution)/shard_map/all_to_all | solution.py:88
  147.8 4.3 %copy.35 = bf16[128,4,2,1024]{3,2,0,1:T(2,128)(2,1)} copy(bf16[128,4,2,1024]{3,2,1,0:T(2,128)(2,1)} %bitcast.20) | data formatting | bytes 4194304 | tf_op jit(solution)/shard_map/all_to_all | solution.py:70
  152.2 4.1 %reshape.295 = bf16[1024,1024]{1,0:T(8,128)(2,1)} reshape(bf16[4,128,2,1024]{3,2,1,0:T(2,128)(2,1)} %bitcast.79) | data formatting | bytes 4194304 | tf_op jit(solution)/shard_map/reshape | solution.py:86
  156.3 19.5 %fusion.16 = (f32[1024]{0:T(1024)S(1)}, f32[1024,1024]{1,0:T(8,128)}) fusion(bf16[4,1024,256]{1,2,0:T(8,128)(2,1)S(1)} %get-tuple-element.34, f32[1024]{0:T(1024)S(1)} %copy-done.3, bf16[1024,2048]{1,0:T(8,128)(2,1)} %param.13, f32[1024,2048]{1,0:T(8,128)} %copy-done.8, bf16[1024,1024]{1,0:T(8,128)(2,1)} %reshape.295, bf16[2048,1024]{1,0:T(8,128)(2,1)} %param.14), kind=kOutput, calls=%fused_computation.27 | convolution fusion | flops 8636070912 | bytes 25174016 | tf_op jit(solution)/shard_map/dot_general | solution.py:33
  175.9 3.6 %fusion.15 = bf16[1024,1024]{1,0:T(8,128)(2,1)S(1)} fusion(bf16[4,1024,256]{1,2,0:T(8,128)(2,1)S(1)} %get-tuple-element.34, bf16[1024,1024]{1,0:T(8,128)(2,1)} %reshape.295, f32[1024,1024]{1,0:T(8,128)} %get-tuple-element.36, f32[1024]{0:T(1024)S(1)} %broadcast_multiply_fusion, f32[1024]{0:T(1024)S(1)} %multiply_multiply_fusion.2, f32[1024]{0:T(1024)S(1)} %copy-done.3, ...), kind=kLoop, calls=%fused_computation.26 | loop fusion | flops 9437184 | bytes 10502144 | tf_op jit(solution)/shard_map/convert_element_type | solution.py:40
  185.4 2.4 collective-permute-start.12
  187.8 3.4 %collective-permute-start.11 = (bf16[1,128,1024]{2,1,0:T(8,128)(2,1)}, bf16[1,128,1024]{2,1,0:T(8,128)(2,1)S(1)}, u32[]{:S(2)}, u32[]{:S(2)}) collective-permute-start(bf16[1,128,1024]{2,1,0:T(8,128)(2,1)} %get-tuple-element.12), channel_id=1, source_target_pairs={{0,5},{1,6},{2,7},{3,8},{4,9},{5,10},{6,11},{7,12},{8,13},{9,14},{... | collective-permute-start | bytes 786440 | tf_op jit(solution)/shard_map/ppermute | solution.py:11
  192.1 4.3 %broadcast_in_dim.54 = f32[16,128,1024]{2,1,0:T(8,128)} broadcast(f32[]{:T(128)} %constant.108.clone.1), dimensions={} | broadcast | bytes 8388612 | tf_op jit(solution)/shard_map/broadcast_in_dim | solution.py:104
  200.1 16.3 %collective-permute-done.8 = bf16[1,128,1024]{2,1,0:T(8,128)(2,1)S(1)} collective-permute-done((bf16[1,128,1024]{2,1,0:T(8,128)(2,1)}, bf16[1,128,1024]{2,1,0:T(8,128)(2,1)S(1)}, u32[]{:S(2)}, u32[]{:S(2)}) %collective-permute-start.8) | collective-permute-done | bytes 262176 | tf_op jit(solution)/shard_map/ppermute | solution.py:11
  219.1 1.9 add_dynamic-update-slice_fusion.4
  221.0 9.1 %collective-permute-done.10 = bf16[1,128,1024]{2,1,0:T(8,128)(2,1)S(1)} collective-permute-done((bf16[1,128,1024]{2,1,0:T(8,128)(2,1)S(1)}, bf16[1,128,1024]{2,1,0:T(8,128)(2,1)S(1)}, u32[]{:S(2)}, u32[]{:S(2)}) %collective-permute-start.10) | collective-permute-done | bytes 262176 | tf_op jit(solution)/shard_map/ppermute | solution.py:11
  233.9 5.3 %copy.28 = bf16[128,4,2,1024]{3,2,1,0:T(2,128)(2,1)} copy(bf16[128,4,2,1024]{3,1,2,0:T(4,128)(2,1)} %bitcast.18) | data formatting | bytes 4194304 | tf_op jit(solution)/shard_map/all_to_all | solution.py:88
  243.0 6.1 %convert_element_type.109 = bf16[16,128,1024]{2,1,0:T(8,128)(2,1)} convert(f32[16,128,1024]{2,1,0:T(8,128)} %add_dynamic-update-slice_fusion) | non-fusion elementwise | flops 2097152 | bytes 12582912 | tf_op jit(solution)/shard_map/convert_element_type | solution.py:114
  (80 shorter events, 35.4 us)
Async XLA Ops:
  0.6 122.5 %copy-start = (bf16[4,256,256]{2,1,0:T(8,128)(2,1)S(1)}, bf16[4,256,256]{2,1,0:T(8,128)(2,1)}, u32[]{:S(2)}) copy-start(bf16[4,256,256]{2,1,0:T(8,128)(2,1)} %param.8) | copy-start | bytes 1572868
  0.6 12.0 %copy-start.4 = (s32[4,2]{0,1:T(2,128)S(1)}, s32[4,2]{0,1:T(2,128)}, u32[]{:S(2)}) copy-start(s32[4,2]{0,1:T(2,128)} %param.9) | copy-start | bytes 100
  0.7 88.6 %copy-start.5 = (s32[4]{0:T(128)S(1)}, s32[4]{0:T(128)}, u32[]{:S(2)}) copy-start(s32[4]{0:T(128)} %param.10) | copy-start | bytes 52
  0.7 137.6 %all-to-all-start.1 = ((bf16[512,2,1024]{2,1,0:T(2,128)(2,1)}), bf16[512,2,1024]{2,1,0:T(2,128)(2,1)}, u32[]{:S(2)}, u32[]{:S(2)}) async-start(bf16[512,2,1024]{2,1,0:T(2,128)(2,1)} %param.15), calls=%async_computation.1 | async-start | bytes 4194304 | tf_op jit(solution)/shard_map/all_to_all | solution.py:70
  81.3 38.5 %collective-permute-start.6 = (bf16[1,128,1024]{2,1,0:T(8,128)(2,1)S(1)}, bf16[1,128,1024]{2,1,0:T(8,128)(2,1)S(1)}, u32[]{:S(2)}, u32[]{:S(2)}) collective-permute-start(bf16[1,128,1024]{2,1,0:T(8,128)(2,1)S(1)} %get-tuple-element.2), channel_id=1, source_target_pairs={{0,121},{1,122},{2,123},{3,124},{4,125},{5,126},{6,127},{7,0},{8,1... | collective-permute-start | bytes 786440 | tf_op jit(solution)/shard_map/ppermute | solution.py:11
  83.2 32.0 %collective-permute-start.4 = (bf16[1,128,1024]{2,1,0:T(8,128)(2,1)S(1)}, bf16[1,128,1024]{2,1,0:T(8,128)(2,1)S(1)}, u32[]{:S(2)}, u32[]{:S(2)}) collective-permute-start(bf16[1,128,1024]{2,1,0:T(8,128)(2,1)S(1)} %get-tuple-element.3), channel_id=1, source_target_pairs={{0,123},{1,124},{2,125},{3,126},{4,127},{5,0},{6,1},{7,2},{8,3},{9... | collective-permute-start | bytes 786440 | tf_op jit(solution)/shard_map/ppermute | solution.py:11
  86.5 27.2 %collective-permute-start.2 = (bf16[1,128,1024]{2,1,0:T(8,128)(2,1)S(1)}, bf16[1,128,1024]{2,1,0:T(8,128)(2,1)S(1)}, u32[]{:S(2)}, u32[]{:S(2)}) collective-permute-start(bf16[1,128,1024]{2,1,0:T(8,128)(2,1)S(1)} %get-tuple-element.5), channel_id=1, source_target_pairs={{0,125},{1,126},{2,127},{3,0},{4,1},{5,2},{6,3},{7,4},{8,5},{9,6},... | collective-permute-start | bytes 786440 | tf_op jit(solution)/shard_map/ppermute | solution.py:11
  88.0 20.8 %collective-permute-start.1 = (bf16[1,128,1024]{2,1,0:T(8,128)(2,1)S(1)}, bf16[1,128,1024]{2,1,0:T(8,128)(2,1)S(1)}, u32[]{:S(2)}, u32[]{:S(2)}) collective-permute-start(bf16[1,128,1024]{2,1,0:T(8,128)(2,1)S(1)} %get-tuple-element.6), channel_id=1, source_target_pairs={{0,126},{1,127},{2,0},{3,1},{4,2},{5,3},{6,4},{7,5},{8,6},{9,7},{1... | collective-permute-start | bytes 786440 | tf_op jit(solution)/shard_map/ppermute | solution.py:11
  88.3 15.4 %collective-permute-start = (bf16[1,128,1024]{2,1,0:T(8,128)(2,1)S(1)}, bf16[1,128,1024]{2,1,0:T(8,128)(2,1)}, u32[]{:S(2)}, u32[]{:S(2)}) collective-permute-start(bf16[1,128,1024]{2,1,0:T(8,128)(2,1)S(1)} %get-tuple-element.7), channel_id=1, source_target_pairs={{0,127},{1,0},{2,1},{3,2},{4,3},{5,4},{6,5},{7,6},{8,7},{9,8},{10,... | collective-permute-start | bytes 786440 | tf_op jit(solution)/shard_map/ppermute | solution.py:11
  103.7 10.7 %collective-permute-start.3 = (bf16[1,128,1024]{2,1,0:T(8,128)(2,1)S(1)}, bf16[1,128,1024]{2,1,0:T(8,128)(2,1)S(1)}, u32[]{:S(2)}, u32[]{:S(2)}) collective-permute-start(bf16[1,128,1024]{2,1,0:T(8,128)(2,1)S(1)} %get-tuple-element.4), channel_id=1, source_target_pairs={{0,124},{1,125},{2,126},{3,127},{4,0},{5,1},{6,2},{7,3},{8,4},{9,5... | collective-permute-start | bytes 786440 | tf_op jit(solution)/shard_map/ppermute | solution.py:11
  108.8 10.3 %collective-permute-start.5 = (bf16[1,128,1024]{2,1,0:T(8,128)(2,1)S(1)}, bf16[1,128,1024]{2,1,0:T(8,128)(2,1)S(1)}, u32[]{:S(2)}, u32[]{:S(2)}) collective-permute-start(bf16[1,128,1024]{2,1,0:T(8,128)(2,1)S(1)} %get-tuple-element.9), channel_id=1, source_target_pairs={{0,122},{1,123},{2,124},{3,125},{4,126},{5,127},{6,0},{7,1},{8,2},... | collective-permute-start | bytes 786440 | tf_op jit(solution)/shard_map/ppermute | solution.py:11
  123.1 2.2 copy-start.7
  125.3 4.5 %copy-start.6 = (bf16[2048,1024]{1,0:T(8,128)(2,1)S(1)}, bf16[2048,1024]{1,0:T(8,128)(2,1)}, u32[]{:S(2)}) copy-start(bf16[2048,1024]{1,0:T(8,128)(2,1)} %param.14) | copy-start | bytes 12582916
  129.8 5.5 %copy-start.8 = (f32[1024,2048]{1,0:T(8,128)}, f32[1024,2048]{1,0:T(8,128)S(1)}, u32[]{:S(2)}) copy-start(f32[1024,2048]{1,0:T(8,128)S(1)} %fusion.53) | copy-start | bytes 25165828
  138.3 95.6 %all-to-all-start = ((bf16[4,256,1024]{2,0,1:T(4,128)(2,1)}), bf16[4,256,1024]{2,0,1:T(4,128)(2,1)}, u32[]{:S(2)}, u32[]{:S(2)}) async-start(bf16[4,256,1024]{2,0,1:T(4,128)(2,1)} %copy.27), calls=%async_computation | async-start | bytes 4194304 | tf_op jit(solution)/shard_map/all_to_all | solution.py:88
  181.6 15.7 %collective-permute-start.7 = (bf16[1,128,1024]{2,1,0:T(8,128)(2,1)}, bf16[1,128,1024]{2,1,0:T(8,128)(2,1)S(1)}, u32[]{:S(2)}, u32[]{:S(2)}) collective-permute-start(bf16[1,128,1024]{2,1,0:T(8,128)(2,1)} %get-tuple-element.16), channel_id=1, source_target_pairs={{0,1},{1,2},{2,3},{3,4},{4,5},{5,6},{6,7},{7,8},{8,9},{9,10},{10,1... | collective-permute-start | bytes 786440 | tf_op jit(solution)/shard_map/ppermute | solution.py:11
  185.1 56.1 %collective-permute-start.13 = (bf16[1,128,1024]{2,1,0:T(8,128)(2,1)}, bf16[1,128,1024]{2,1,0:T(8,128)(2,1)S(1)}, u32[]{:S(2)}, u32[]{:S(2)}) collective-permute-start(bf16[1,128,1024]{2,1,0:T(8,128)(2,1)} %get-tuple-element.10), channel_id=1, source_target_pairs={{0,7},{1,8},{2,9},{3,10},{4,11},{5,12},{6,13},{7,14},{8,15},{9,16}... | collective-permute-start | bytes 786440 | tf_op jit(solution)/shard_map/ppermute | solution.py:11
  185.4 53.8 %collective-permute-start.12 = (bf16[1,128,1024]{2,1,0:T(8,128)(2,1)}, bf16[1,128,1024]{2,1,0:T(8,128)(2,1)S(1)}, u32[]{:S(2)}, u32[]{:S(2)}) collective-permute-start(bf16[1,128,1024]{2,1,0:T(8,128)(2,1)} %get-tuple-element.11), channel_id=1, source_target_pairs={{0,6},{1,7},{2,8},{3,9},{4,10},{5,11},{6,12},{7,13},{8,14},{9,15},... | collective-permute-start | bytes 786440 | tf_op jit(solution)/shard_map/ppermute | solution.py:11
  187.8 44.2 %collective-permute-start.11 = (bf16[1,128,1024]{2,1,0:T(8,128)(2,1)}, bf16[1,128,1024]{2,1,0:T(8,128)(2,1)S(1)}, u32[]{:S(2)}, u32[]{:S(2)}) collective-permute-start(bf16[1,128,1024]{2,1,0:T(8,128)(2,1)} %get-tuple-element.12), channel_id=1, source_target_pairs={{0,5},{1,6},{2,7},{3,8},{4,9},{5,10},{6,11},{7,12},{8,13},{9,14},{... | collective-permute-start | bytes 786440 | tf_op jit(solution)/shard_map/ppermute | solution.py:11
  191.2 6.1 %copy-start.2 = (bf16[1,128,1024]{2,1,0:T(8,128)(2,1)S(1)}, bf16[1,128,1024]{2,1,0:T(8,128)(2,1)}, u32[]{:S(2)}) copy-start(bf16[1,128,1024]{2,1,0:T(8,128)(2,1)} %get-tuple-element.14) | copy-start | bytes 786436
  191.2 25.2 %copy-start.1 = (bf16[1,128,1024]{2,1,0:T(8,128)(2,1)S(1)}, bf16[1,128,1024]{2,1,0:T(8,128)(2,1)}, u32[]{:S(2)}) copy-start(bf16[1,128,1024]{2,1,0:T(8,128)(2,1)} %get-tuple-element.13) | copy-start | bytes 786436
  191.2 25.2 %collective-permute-start.8 = (bf16[1,128,1024]{2,1,0:T(8,128)(2,1)}, bf16[1,128,1024]{2,1,0:T(8,128)(2,1)S(1)}, u32[]{:S(2)}, u32[]{:S(2)}) collective-permute-start(bf16[1,128,1024]{2,1,0:T(8,128)(2,1)} %get-tuple-element.15), channel_id=1, source_target_pairs={{0,2},{1,3},{2,4},{3,5},{4,6},{5,7},{6,8},{7,9},{8,10},{9,11},{10,... | collective-permute-start | bytes 786440 | tf_op jit(solution)/shard_map/ppermute | solution.py:11
  197.3 21.8 %collective-permute-start.9 = (bf16[1,128,1024]{2,1,0:T(8,128)(2,1)S(1)}, bf16[1,128,1024]{2,1,0:T(8,128)(2,1)S(1)}, u32[]{:S(2)}, u32[]{:S(2)}) collective-permute-start(bf16[1,128,1024]{2,1,0:T(8,128)(2,1)S(1)} %copy-done.2), channel_id=1, source_target_pairs={{0,3},{1,4},{2,5},{3,6},{4,7},{5,8},{6,9},{7,10},{8,11},{9,12},{10... | collective-permute-start | bytes 786440 | tf_op jit(solution)/shard_map/ppermute | solution.py:11
  216.4 13.7 %collective-permute-start.10 = (bf16[1,128,1024]{2,1,0:T(8,128)(2,1)S(1)}, bf16[1,128,1024]{2,1,0:T(8,128)(2,1)S(1)}, u32[]{:S(2)}, u32[]{:S(2)}) collective-permute-start(bf16[1,128,1024]{2,1,0:T(8,128)(2,1)S(1)} %copy-done.1), channel_id=1, source_target_pairs={{0,4},{1,5},{2,6},{3,7},{4,8},{5,9},{6,10},{7,11},{8,12},{9,13},{1... | collective-permute-start | bytes 786440 | tf_op jit(solution)/shard_map/ppermute | solution.py:11
  (1 other events, 1.2 us)
where the time goes:
time: 250 us; the launch traced here: 249 us
  blocking collectives  49.1 us (20%)
  starting transfers between devices  46.3 us (19%)
  local copies, waits for them, and re-layouts  36.1 us (14%)
  matrix products  31.3 us (13%)
  between operations  30.9 us (12%)
  waiting for transfers between devices  30.3 us (12%)
  other arithmetic  25 us (10%)
    all_gather x1, blocking collectives, on_device(): all_lists = lax.all_gather(flat_lists, 'dp', axis=0, tiled=False)  49.1 us
    ppermute x14, waiting for transfers between devices, from_behind(): lax.ppermute(array, axis, [(i, (i + by) % count) for i in range(count)])  30.3 us
    ppermute x14, starting transfers between devices, from_behind(): lax.ppermute(array, axis, [(i, (i + by) % count) for i in range(count)])  24.8 us
    dot_general x1, matrix products, encode_rows(): lax.dot_general(grad_hidden, w_in, (((1,), (1,)), ((), ())), preferred_el...  19.5 us
    dynamic_update_slice x8, other arithmetic, on_device(): lax.dynamic_update_slice_in_dim(total, current + piece.astype(jnp.float32...  14.2 us
    all_to_all x1, starting transfers between devices, on_device(): lax.all_to_all(cotangent, 'dp', split_axis=0, concat_axis=1, tiled=True)  12 us
    all_to_all x1, starting transfers between devices, on_device(): lax.all_to_all(encoded.reshape(sessions_here, bins_all, latent_width), 'd...  9.52 us
    unnamed x27, local copies, waits for them, and re-layouts  6.21 us
  transfers between devices with their start and end apart: 16, of which 5 were waited for; matrix products, arithmetic and copies ran while one was open for 34% of the time, Pallas kernels for 0%

commit v1 on v0

--- a/solution.py
+++ b/solution.py
@@ -29,7 +29,7 @@
     grad_activated = lax.dot_general(
         cot_rows, w_out, (((1,), (1,)), ((), ())), preferred_element_type=jnp.float32
     )
-    grad_hidden = pullback(grad_activated)[0].astype(jnp.bfloat16)
+    grad_hidden = lax.optimization_barrier(pullback(grad_activated)[0].astype(jnp.bfloat16))
     grad_normed = lax.dot_general(
         grad_hidden, w_in, (((1,), (1,)), ((), ())), preferred_element_type=jnp.float32
     )
@@ -56,9 +56,14 @@
     match = offsets[None, :] == jnp.arange(near, dtype=jnp.int32)[:, None]
     slot_of = jnp.sum(jnp.where(match, slot_ids[None, :], 0), axis=1)
 
-    all_lists = lax.all_gather(flat_lists, "dp", axis=0, tiled=False)
-    sources = jnp.mod(me - jnp.arange(near, dtype=jnp.int32), devices)
-    source_lists = jnp.take(all_lists, sources, axis=0)
+    source_lists = flat_lists[None, :]
+    span = 1
+    while span < near:
+        source_lists = jnp.concatenate(
+            [source_lists, from_behind(source_lists, "dp", span)], axis=0
+        )
+        span *= 2
+    source_lists = source_lists[:near]
     mine = (source_lists // table_rows) == me
     rows_in = jnp.sum(jnp.where(mine, jnp.mod(source_lists, table_rows), 0), axis=1)
 

time: 250 us -> 258 us (1.032); the launches traced: 249 us -> 254 us
  waiting for transfers between devices: 30.3 us -> 101 us
  blocking collectives: 49.1 us -> 0 us
  other arithmetic: 25 us -> 8.28 us
  local copies, waits for them, and re-layouts: 36.1 us -> 30.4 us
  matrix products: 31.3 us -> 34.5 us
  starting transfers between devices: 46.3 us -> 49.2 us
    ppermute x14 -> x17, waiting for transfers between devices: 30.3 us -> 101 us  [from_behind(): lax.ppermute(array, axis, [(i, (i + by) % count) for i in range(count)])]
    all_gather x1 -> x0, blocking collectives: 49.1 us -> none  [on_device(): all_lists = lax.all_gather(flat_lists, 'dp', axis=0, tiled=False)]
    dot_general x1, matrix products: 19.5 us -> 4.72 us  [encode_rows(): lax.dot_general(grad_hidden, w_in, (((1,), (1,)), ((), ())), preferred_el...]
    dynamic_update_slice x8, other arithmetic: 14.2 us -> 1.63 us  [on_device(): lax.dynamic_update_slice_in_dim(total, current + piece.astype(jnp.float32...]
    dot_general x0 -> x1, matrix products: none -> 7.15 us  [encode_rows(): lax.dot_general(cot_rows, w_out, (((1,), (1,)), ((), ())), preferred_elem...]
    dot_general x1, matrix products: 4.49 us -> 11 us  [encode_rows(): hidden_pre = jnp.dot(normed, w_in, preferred_element_type=jnp.float32)]
    ppermute x14 -> x17, starting transfers between devices: 24.8 us -> 29.9 us  [from_behind(): lax.ppermute(array, axis, [(i, (i + by) % count) for i in range(count)])]
    convert_element_type x1, other arithmetic: 6.06 us -> 2.67 us  [on_device(): return (encoded_out, total.astype(jnp.bfloat16))]
  transfers between devices with their start and end apart: 16 -> 19, of which waited for: 5 -> 8; matrix products, arithmetic and copies ran while one was open for 34% -> 9% of each run, Pallas kernels for 0% -> 0%
where the time goes in v1:
time: 258 us; the launch traced here: 254 us
  waiting for transfers between devices  101 us (39%)
  starting transfers between devices  49.2 us (19%)
  matrix products  34.5 us (13%)
  between operations  31.1 us (12%)
  local copies, waits for them, and re-layouts  30.4 us (12%)
  other arithmetic  8.28 us (3%)
    ppermute x17, waiting for transfers between devices, from_behind(): lax.ppermute(array, axis, [(i, (i + by) % count) for i in range(count)])  101 us
    ppermute x17, starting transfers between devices, from_behind(): lax.ppermute(array, axis, [(i, (i + by) % count) for i in range(count)])  29.9 us
    all_to_all x1, starting transfers between devices, on_device(): lax.all_to_all(cotangent, 'dp', split_axis=0, concat_axis=1, tiled=True)  12 us
    dot_general x1, matrix products, encode_rows(): hidden_pre = jnp.dot(normed, w_in, preferred_element_type=jnp.float32)  11 us
    dot_general x1, matrix products, encode_rows(): jnp.dot(activated, w_out, preferred_element_type=jnp.float32)  8.6 us
    all_to_all x1, starting transfers between devices, on_device(): lax.all_to_all(encoded.reshape(sessions_here, bins_all, latent_width), 'd...  7.35 us
    dot_general x1, matrix products, encode_rows(): lax.dot_general(cot_rows, w_out, (((1,), (1,)), ((), ())), preferred_elem...  7.15 us
  transfers between devices with their start and end apart: 19, of which 8 were waited for; matrix products, arithmetic and copies ran while one was open for 9% of the time, Pallas kernels for 0%

profile of v1, /device:TPU:1, one launch (start us, length us, event | category | flops | bytes accessed | tf_op | source)
XLA Modules:
  0.0 254.0 jit_solution(3689127220873655251)
XLA Ops:
  0.7 12.0 %all-to-all-start.1 = ((bf16[512,2,1024]{2,1,0:T(2,128)(2,1)}), bf16[512,2,1024]{2,1,0:T(2,128)(2,1)}, u32[]{:S(2)}, u32[]{:S(2)}) async-start(bf16[512,2,1024]{2,1,0:T(2,128)(2,1)} %param.15), calls=%async_computation.1 | async-start | bytes 4194304 | tf_op jit(solution)/shard_map/all_to_all | solution.py:75
  14.7 18.7 %collective-permute-done = s32[1,8]{1,0:T(1,128)S(1)} collective-permute-done((s32[1,8]{1,0:T(1,128)S(1)}, s32[1,8]{1,0:T(1,128)S(1)}, u32[]{:S(2)}, u32[]{:S(2)}) %collective-permute-start) | collective-permute-done | bytes 64 | tf_op jit(solution)/shard_map/ppermute | solution.py:11
  34.5 6.8 %collective-permute-done.1 = s32[2,8]{1,0:T(2,128)S(1)} collective-permute-done((s32[2,8]{1,0:T(2,128)S(1)}, s32[2,8]{1,0:T(2,128)S(1)}, u32[]{:S(2)}, u32[]{:S(2)}) %collective-permute-start.1) | collective-permute-done | bytes 96 | tf_op jit(solution)/shard_map/ppermute | solution.py:11
  41.5 8.1 %collective-permute-done.2 = s32[4,8]{1,0:T(4,128)S(1)} collective-permute-done((s32[4,8]{1,0:T(4,128)S(1)}, s32[4,8]{1,0:T(4,128)S(1)}, u32[]{:S(2)}, u32[]{:S(2)}) %collective-permute-start.2) | collective-permute-done | bytes 160 | tf_op jit(solution)/shard_map/ppermute | solution.py:11
  65.5 2.5 constant_dynamic-slice_fusion.7
  68.0 10.6 %collective-permute-start.3 = (bf16[1,128,1024]{2,1,0:T(8,128)(2,1)S(1)}, bf16[1,128,1024]{2,1,0:T(8,128)(2,1)S(1)}, u32[]{:S(2)}, u32[]{:S(2)}) collective-permute-start(bf16[1,128,1024]{2,1,0:T(8,128)(2,1)S(1)} %get-tuple-element.7), channel_id=1, source_target_pairs={{0,127},{1,0},{2,1},{3,2},{4,3},{5,4},{6,5},{7,6},{8,7},{9,8},{10,... | collective-permute-start | bytes 786440 | tf_op jit(solution)/shard_map/ppermute | solution.py:11
  95.1 25.4 %collective-permute-done.6 = bf16[1,128,1024]{2,1,0:T(8,128)(2,1)S(1)} collective-permute-done((bf16[1,128,1024]{2,1,0:T(8,128)(2,1)S(1)}, bf16[1,128,1024]{2,1,0:T(8,128)(2,1)S(1)}, u32[]{:S(2)}, u32[]{:S(2)}) %collective-permute-start.6) | collective-permute-done | bytes 262176 | tf_op jit(solution)/shard_map/ppermute | solution.py:11
  128.8 4.3 %copy.33 = bf16[128,4,2,1024]{3,2,0,1:T(2,128)(2,1)} copy(bf16[128,4,2,1024]{3,2,1,0:T(2,128)(2,1)} %bitcast.18) | data formatting | bytes 4194304 | tf_op jit(solution)/shard_map/all_to_all | solution.py:75
  133.1 4.1 %reshape.241 = bf16[1024,1024]{1,0:T(8,128)(2,1)} reshape(bf16[4,128,2,1024]{3,2,1,0:T(2,128)(2,1)} %bitcast.78) | data formatting | bytes 4194304 | tf_op jit(solution)/shard_map/reshape | solution.py:91
  137.2 7.1 %fusion.40 = f32[1024,2048]{1,0:T(8,128)S(1)} fusion(bf16[1024,1024]{1,0:T(8,128)(2,1)} %reshape.241, bf16[2048,1024]{1,0:T(8,128)(2,1)} %param.14), kind=kOutput, calls=%fused_computation.121 | convolution fusion | flops 4294967296 | bytes 14680064 | tf_op jit(solution)/shard_map/dot_general | solution.py:29
  144.4 11.0 %fusion.6 = (bf16[1024,2048]{1,0:T(8,128)(2,1)S(1)}, f32[1024,2048]{1,0:T(8,128)}) fusion(f32[1024,2048]{1,0:T(8,128)S(1)} %fusion.40, bf16[1024,1024]{1,0:T(8,128)(2,1)S(1)} %copy-done.2, bf16[1024,2048]{1,0:T(8,128)(2,1)S(1)} %copy-done.8), kind=kOutput, calls=%fused_computation.9 | convolution fusion | flops 4336910336 | bytes 27262976 | tf_op jit(solution)/shard_map/dot_general | solution.py:23
  155.4 4.7 %fusion.16 = (f32[1024]{0:T(1024)S(1)}, f32[1024,1024]{1,0:T(8,128)S(1)}) fusion(bf16[4,1024,256]{1,2,0:T(8,128)(2,1)S(1)} %get-tuple-element.34, f32[1024]{0:T(1024)S(1)} %copy-done.5, bf16[1024,2048]{1,0:T(8,128)(2,1)S(1)} %get-tuple-element.35, bf16[1024,2048]{1,0:T(8,128)(2,1)S(1)} %copy-done.8), kind=kOutput, calls=%fused_computation.26 | convolution fusion | flops 4299160576 | bytes 14688256 | tf_op jit(solution)/shard_map/dot_general | solution.py:33
  160.1 8.6 %fusion.11 = bf16[1024,1024]{1,0:T(8,128)(2,1)S(1)} fusion(bf16[4,1024,256]{1,2,0:T(8,128)(2,1)S(1)} %get-tuple-element.34, bf16[2048,1024]{1,0:T(8,128)(2,1)S(1)} %copy-done.9, f32[1024,2048]{1,0:T(8,128)} %get-tuple-element.36), kind=kOutput, calls=%fused_computation.21 | convolution fusion | flops 4316987392 | bytes 16777216 | tf_op jit(solution)/shard_map/dot_general | solution.py:26
  168.7 2.9 %copy.25 = bf16[4,256,1024]{2,0,1:T(4,128)(2,1)} copy(bf16[4,256,1024]{2,1,0:T(8,128)(2,1)S(1)} %bitcast.80) | data formatting | bytes 4194304 | tf_op jit(solution)/shard_map/reshape | solution.py:94
  175.4 7.3 %all-to-all-start = ((bf16[4,256,1024]{2,0,1:T(4,128)(2,1)}), bf16[4,256,1024]{2,0,1:T(4,128)(2,1)S(1)}, u32[]{:S(2)}, u32[]{:S(2)}) async-start(bf16[4,256,1024]{2,0,1:T(4,128)(2,1)} %copy.25), calls=%async_computation | async-start | bytes 4194304 | tf_op jit(solution)/shard_map/all_to_all | solution.py:93
  182.7 2.5 constant_dynamic-slice_fusion
  189.1 2.4 collective-permute-start.15
  191.5 3.3 %collective-permute-start.14 = (bf16[1,128,1024]{2,1,0:T(8,128)(2,1)}, bf16[1,128,1024]{2,1,0:T(8,128)(2,1)S(1)}, u32[]{:S(2)}, u32[]{:S(2)}) collective-permute-start(bf16[1,128,1024]{2,1,0:T(8,128)(2,1)} %get-tuple-element.12), channel_id=1, source_target_pairs={{0,5},{1,6},{2,7},{3,8},{4,9},{5,10},{6,11},{7,12},{8,13},{9,14},{... | collective-permute-start | bytes 786440 | tf_op jit(solution)/shard_map/ppermute | solution.py:11
  197.9 11.8 %collective-permute-done.10 = bf16[1,128,1024]{2,1,0:T(8,128)(2,1)S(1)} collective-permute-done((bf16[1,128,1024]{2,1,0:T(8,128)(2,1)}, bf16[1,128,1024]{2,1,0:T(8,128)(2,1)S(1)}, u32[]{:S(2)}, u32[]{:S(2)}) %collective-permute-start.10) | collective-permute-done | bytes 262176 | tf_op jit(solution)/shard_map/ppermute | solution.py:11
  209.6 7.6 %collective-permute-start.12 = (bf16[1,128,1024]{2,1,0:T(8,128)(2,1)S(1)}, bf16[1,128,1024]{2,1,0:T(8,128)(2,1)S(1)}, u32[]{:S(2)}, u32[]{:S(2)}) collective-permute-start(bf16[1,128,1024]{2,1,0:T(8,128)(2,1)S(1)} %copy-done.4), channel_id=1, source_target_pairs={{0,3},{1,4},{2,5},{3,6},{4,7},{5,8},{6,9},{7,10},{8,11},{9,12},{10... | collective-permute-start | bytes 786440 | tf_op jit(solution)/shard_map/ppermute | solution.py:11
  217.4 18.9 %collective-permute-done.11 = bf16[1,128,1024]{2,1,0:T(8,128)(2,1)S(1)} collective-permute-done((bf16[1,128,1024]{2,1,0:T(8,128)(2,1)}, bf16[1,128,1024]{2,1,0:T(8,128)(2,1)S(1)}, u32[]{:S(2)}, u32[]{:S(2)}) %collective-permute-start.11) | collective-permute-done | bytes 262176 | tf_op jit(solution)/shard_map/ppermute | solution.py:11
  237.3 10.0 %collective-permute-done.13 = bf16[1,128,1024]{2,1,0:T(8,128)(2,1)S(1)} collective-permute-done((bf16[1,128,1024]{2,1,0:T(8,128)(2,1)S(1)}, bf16[1,128,1024]{2,1,0:T(8,128)(2,1)S(1)}, u32[]{:S(2)}, u32[]{:S(2)}) %collective-permute-start.13) | collective-permute-done | bytes 262176 | tf_op jit(solution)/shard_map/ppermute | solution.py:11
  247.7 2.7 %convert_element_type.109 = bf16[16,128,1024]{2,1,0:T(8,128)(2,1)} convert(f32[16,128,1024]{2,1,0:T(8,128)S(1)} %add_dynamic-update-slice_fusion) | non-fusion elementwise | flops 2097152 | bytes 12582912 | tf_op jit(solution)/shard_map/convert_element_type | solution.py:119
  250.3 3.7 %copy.26 = bf16[128,4,2,1024]{3,2,1,0:T(2,128)(2,1)} copy(bf16[128,4,2,1024]{3,1,2,0:T(4,128)(2,1)S(1)} %bitcast.75) | data formatting | bytes 4194304 | tf_op jit(solution)/shard_map/all_to_all | solution.py:93
  (86 shorter events, 25.7 us)
Async XLA Ops:
  0.6 125.4 %copy-start = (bf16[4,256,256]{2,1,0:T(8,128)(2,1)S(1)}, bf16[4,256,256]{2,1,0:T(8,128)(2,1)}, u32[]{:S(2)}) copy-start(bf16[4,256,256]{2,1,0:T(8,128)(2,1)} %param.8) | copy-start | bytes 1572868
  0.6 12.0 %copy-start.6 = (s32[4,2]{0,1:T(2,128)S(1)}, s32[4,2]{0,1:T(2,128)}, u32[]{:S(2)}) copy-start(s32[4,2]{0,1:T(2,128)} %param.9) | copy-start | bytes 100
  0.7 14.0 %copy-start.7 = (s32[4]{0:T(128)S(1)}, s32[4]{0:T(128)}, u32[]{:S(2)}) copy-start(s32[4]{0:T(128)} %param.10) | copy-start | bytes 52
  0.7 128.1 %all-to-all-start.1 = ((bf16[512,2,1024]{2,1,0:T(2,128)(2,1)}), bf16[512,2,1024]{2,1,0:T(2,128)(2,1)}, u32[]{:S(2)}, u32[]{:S(2)}) async-start(bf16[512,2,1024]{2,1,0:T(2,128)(2,1)} %param.15), calls=%async_computation.1 | async-start | bytes 4194304 | tf_op jit(solution)/shard_map/all_to_all | solution.py:75
  12.8 20.6 %collective-permute-start = (s32[1,8]{1,0:T(1,128)S(1)}, s32[1,8]{1,0:T(1,128)S(1)}, u32[]{:S(2)}, u32[]{:S(2)}) collective-permute-start(s32[1,8]{1,0:T(1,128)S(1)} %broadcast_in_dim_reshape.5), channel_id=1, source_target_pairs={{0,1},{1,2},{2,3},{3,4},{4,5},{5,6},{6,7},{7,8},{8,9},{9,10},{10,1... | collective-permute-start | bytes 104 | tf_op jit(solution)/shard_map/ppermute | solution.py:11
  33.4 8.0 %collective-permute-start.1 = (s32[2,8]{1,0:T(2,128)S(1)}, s32[2,8]{1,0:T(2,128)S(1)}, u32[]{:S(2)}, u32[]{:S(2)}) collective-permute-start(s32[2,8]{1,0:T(2,128)S(1)} %pad_add_fusion.2), channel_id=1, source_target_pairs={{0,2},{1,3},{2,4},{3,5},{4,6},{5,7},{6,8},{7,9},{8,10},{9,11},{10,... | collective-permute-start | bytes 200 | tf_op jit(solution)/shard_map/ppermute | solution.py:11
  41.4 8.2 %collective-permute-start.2 = (s32[4,8]{1,0:T(4,128)S(1)}, s32[4,8]{1,0:T(4,128)S(1)}, u32[]{:S(2)}, u32[]{:S(2)}) collective-permute-start(s32[4,8]{1,0:T(4,128)S(1)} %pad_add_fusion.1), channel_id=1, source_target_pairs={{0,4},{1,5},{2,6},{3,7},{4,8},{5,9},{6,10},{7,11},{8,12},{9,13},{1... | collective-permute-start | bytes 392 | tf_op jit(solution)/shard_map/ppermute | solution.py:11
  68.0 24.8 %collective-permute-start.3 = (bf16[1,128,1024]{2,1,0:T(8,128)(2,1)S(1)}, bf16[1,128,1024]{2,1,0:T(8,128)(2,1)S(1)}, u32[]{:S(2)}, u32[]{:S(2)}) collective-permute-start(bf16[1,128,1024]{2,1,0:T(8,128)(2,1)S(1)} %get-tuple-element.7), channel_id=1, source_target_pairs={{0,127},{1,0},{2,1},{3,2},{4,3},{5,4},{6,5},{7,6},{8,7},{9,8},{10,... | collective-permute-start | bytes 786440 | tf_op jit(solution)/shard_map/ppermute | solution.py:11
  78.8 14.9 %collective-permute-start.4 = (bf16[1,128,1024]{2,1,0:T(8,128)(2,1)S(1)}, bf16[1,128,1024]{2,1,0:T(8,128)(2,1)S(1)}, u32[]{:S(2)}, u32[]{:S(2)}) collective-permute-start(bf16[1,128,1024]{2,1,0:T(8,128)(2,1)S(1)} %get-tuple-element.6), channel_id=1, source_target_pairs={{0,126},{1,127},{2,0},{3,1},{4,2},{5,3},{6,4},{7,5},{8,6},{9,7},{1... | collective-permute-start | bytes 786440 | tf_op jit(solution)/shard_map/ppermute | solution.py:11
  79.5 14.9 %collective-permute-start.5 = (bf16[1,128,1024]{2,1,0:T(8,128)(2,1)S(1)}, bf16[1,128,1024]{2,1,0:T(8,128)(2,1)S(1)}, u32[]{:S(2)}, u32[]{:S(2)}) collective-permute-start(bf16[1,128,1024]{2,1,0:T(8,128)(2,1)S(1)} %get-tuple-element.5), channel_id=1, source_target_pairs={{0,125},{1,126},{2,127},{3,0},{4,1},{5,2},{6,3},{7,4},{8,5},{9,6},... | collective-permute-start | bytes 786440 | tf_op jit(solution)/shard_map/ppermute | solution.py:11
  92.7 30.0 %collective-permute-start.9 = (bf16[1,128,1024]{2,1,0:T(8,128)(2,1)S(1)}, bf16[1,128,1024]{2,1,0:T(8,128)(2,1)S(1)}, u32[]{:S(2)}, u32[]{:S(2)}) collective-permute-start(bf16[1,128,1024]{2,1,0:T(8,128)(2,1)S(1)} %get-tuple-element.2), channel_id=1, source_target_pairs={{0,121},{1,122},{2,123},{3,124},{4,125},{5,126},{6,127},{7,0},{8,1... | collective-permute-start | bytes 786440 | tf_op jit(solution)/shard_map/ppermute | solution.py:11
  92.8 28.5 %collective-permute-start.7 = (bf16[1,128,1024]{2,1,0:T(8,128)(2,1)S(1)}, bf16[1,128,1024]{2,1,0:T(8,128)(2,1)S(1)}, u32[]{:S(2)}, u32[]{:S(2)}) collective-permute-start(bf16[1,128,1024]{2,1,0:T(8,128)(2,1)S(1)} %get-tuple-element.3), channel_id=1, source_target_pairs={{0,123},{1,124},{2,125},{3,126},{4,127},{5,0},{6,1},{7,2},{8,3},{9... | collective-permute-start | bytes 786440 | tf_op jit(solution)/shard_map/ppermute | solution.py:11
  92.9 27.6 %collective-permute-start.6 = (bf16[1,128,1024]{2,1,0:T(8,128)(2,1)S(1)}, bf16[1,128,1024]{2,1,0:T(8,128)(2,1)S(1)}, u32[]{:S(2)}, u32[]{:S(2)}) collective-permute-start(bf16[1,128,1024]{2,1,0:T(8,128)(2,1)S(1)} %get-tuple-element.4), channel_id=1, source_target_pairs={{0,124},{1,125},{2,126},{3,127},{4,0},{5,1},{6,2},{7,3},{8,4},{9,5... | collective-permute-start | bytes 786440 | tf_op jit(solution)/shard_map/ppermute | solution.py:11
  93.7 28.3 %collective-permute-start.8 = (bf16[1,128,1024]{2,1,0:T(8,128)(2,1)S(1)}, bf16[1,128,1024]{2,1,0:T(8,128)(2,1)S(1)}, u32[]{:S(2)}, u32[]{:S(2)}) collective-permute-start(bf16[1,128,1024]{2,1,0:T(8,128)(2,1)S(1)} %get-tuple-element.9), channel_id=1, source_target_pairs={{0,122},{1,123},{2,124},{3,125},{4,126},{5,127},{6,0},{7,1},{8,2},... | collective-permute-start | bytes 786440 | tf_op jit(solution)/shard_map/ppermute | solution.py:11
  175.4 75.0 %all-to-all-start = ((bf16[4,256,1024]{2,0,1:T(4,128)(2,1)}), bf16[4,256,1024]{2,0,1:T(4,128)(2,1)S(1)}, u32[]{:S(2)}, u32[]{:S(2)}) async-start(bf16[4,256,1024]{2,0,1:T(4,128)(2,1)} %copy.25), calls=%async_computation | async-start | bytes 4194304 | tf_op jit(solution)/shard_map/all_to_all | solution.py:93
  185.2 24.4 %collective-permute-start.10 = (bf16[1,128,1024]{2,1,0:T(8,128)(2,1)}, bf16[1,128,1024]{2,1,0:T(8,128)(2,1)S(1)}, u32[]{:S(2)}, u32[]{:S(2)}) collective-permute-start(bf16[1,128,1024]{2,1,0:T(8,128)(2,1)} %get-tuple-element.16), channel_id=1, source_target_pairs={{0,1},{1,2},{2,3},{3,4},{4,5},{5,6},{6,7},{7,8},{8,9},{9,10},{10,1... | collective-permute-start | bytes 786440 | tf_op jit(solution)/shard_map/ppermute | solution.py:11
  188.8 58.8 %collective-permute-start.16 = (bf16[1,128,1024]{2,1,0:T(8,128)(2,1)S(1)}, bf16[1,128,1024]{2,1,0:T(8,128)(2,1)S(1)}, u32[]{:S(2)}, u32[]{:S(2)}) collective-permute-start(bf16[1,128,1024]{2,1,0:T(8,128)(2,1)S(1)} %get-tuple-element.10), channel_id=1, source_target_pairs={{0,7},{1,8},{2,9},{3,10},{4,11},{5,12},{6,13},{7,14},{8,15},{9,16}... | collective-permute-start | bytes 786440 | tf_op jit(solution)/shard_map/ppermute | solution.py:11
  189.1 58.3 %collective-permute-start.15 = (bf16[1,128,1024]{2,1,0:T(8,128)(2,1)S(1)}, bf16[1,128,1024]{2,1,0:T(8,128)(2,1)S(1)}, u32[]{:S(2)}, u32[]{:S(2)}) collective-permute-start(bf16[1,128,1024]{2,1,0:T(8,128)(2,1)S(1)} %get-tuple-element.11), channel_id=1, source_target_pairs={{0,6},{1,7},{2,8},{3,9},{4,10},{5,11},{6,12},{7,13},{8,14},{9,15},... | collective-permute-start | bytes 786440 | tf_op jit(solution)/shard_map/ppermute | solution.py:11
  191.5 55.8 %collective-permute-start.14 = (bf16[1,128,1024]{2,1,0:T(8,128)(2,1)}, bf16[1,128,1024]{2,1,0:T(8,128)(2,1)S(1)}, u32[]{:S(2)}, u32[]{:S(2)}) collective-permute-start(bf16[1,128,1024]{2,1,0:T(8,128)(2,1)} %get-tuple-element.12), channel_id=1, source_target_pairs={{0,5},{1,6},{2,7},{3,8},{4,9},{5,10},{6,11},{7,12},{8,13},{9,14},{... | collective-permute-start | bytes 786440 | tf_op jit(solution)/shard_map/ppermute | solution.py:11
  194.9 14.7 %copy-start.4 = (bf16[1,128,1024]{2,1,0:T(8,128)(2,1)S(1)}, bf16[1,128,1024]{2,1,0:T(8,128)(2,1)}, u32[]{:S(2)}) copy-start(bf16[1,128,1024]{2,1,0:T(8,128)(2,1)} %get-tuple-element.14) | copy-start | bytes 786436
  194.9 41.3 %copy-start.3 = (bf16[1,128,1024]{2,1,0:T(8,128)(2,1)S(1)}, bf16[1,128,1024]{2,1,0:T(8,128)(2,1)}, u32[]{:S(2)}) copy-start(bf16[1,128,1024]{2,1,0:T(8,128)(2,1)} %get-tuple-element.13) | copy-start | bytes 786436
  194.9 41.3 %collective-permute-start.11 = (bf16[1,128,1024]{2,1,0:T(8,128)(2,1)}, bf16[1,128,1024]{2,1,0:T(8,128)(2,1)S(1)}, u32[]{:S(2)}, u32[]{:S(2)}) collective-permute-start(bf16[1,128,1024]{2,1,0:T(8,128)(2,1)} %get-tuple-element.15), channel_id=1, source_target_pairs={{0,2},{1,3},{2,4},{3,5},{4,6},{5,7},{6,8},{7,9},{8,10},{9,11},{10,... | collective-permute-start | bytes 786440 | tf_op jit(solution)/shard_map/ppermute | solution.py:11
  209.6 27.5 %collective-permute-start.12 = (bf16[1,128,1024]{2,1,0:T(8,128)(2,1)S(1)}, bf16[1,128,1024]{2,1,0:T(8,128)(2,1)S(1)}, u32[]{:S(2)}, u32[]{:S(2)}) collective-permute-start(bf16[1,128,1024]{2,1,0:T(8,128)(2,1)S(1)} %copy-done.4), channel_id=1, source_target_pairs={{0,3},{1,4},{2,5},{3,6},{4,7},{5,8},{6,9},{7,10},{8,11},{9,12},{10... | collective-permute-start | bytes 786440 | tf_op jit(solution)/shard_map/ppermute | solution.py:11
  236.2 11.0 %collective-permute-start.13 = (bf16[1,128,1024]{2,1,0:T(8,128)(2,1)S(1)}, bf16[1,128,1024]{2,1,0:T(8,128)(2,1)S(1)}, u32[]{:S(2)}, u32[]{:S(2)}) collective-permute-start(bf16[1,128,1024]{2,1,0:T(8,128)(2,1)S(1)} %copy-done.3), channel_id=1, source_target_pairs={{0,4},{1,5},{2,6},{3,7},{4,8},{5,9},{6,10},{7,11},{8,12},{9,13},{1... | collective-permute-start | bytes 786440 | tf_op jit(solution)/shard_map/ppermute | solution.py:11
  (5 other events, 23.2 us)
